TPU v7x, 32 devices: a whole 2x2x4 slice. The times are simulated.
32 devices in a mesh: var: 8 (over z, y), samp: 4 (over x, core).
Axes of the slice: x: 2, y: 2, z: 4, core: 2. Of those that a mesh axis runs over, the one named last changes fastest.
Arguments:
- dosages: bfloat16 [8192, 6144], P('samp', 'var'), may hold values from 0 to 2
- observed: int32 [8192, 6144], P('samp', 'var'), may hold values 0 or 1
Outputs:
- ld_scores: float32 [6144], P(('var', 'samp'))
All inputs are finite; a program needn't handle non-finite values. No bound on the sum of `observed` on one device may be relied on, other than what follows from the above.
Results may differ from a plain program's by a relative error of at most 0.00055.
Values may be sent and summed in bfloat16 or wider, within the bound.
No kernel may reach another device: no remote copies, remote signals or barrier semaphores. Data moves between devices by JAX's collectives and lax.ppermute only.
A program may use at most 192 MiB of HBM per device.

v0:
```python
import jax
import jax.numpy as jnp
from jax import lax
from jax.sharding import PartitionSpec as P

BAND = 3
PARTNER_STEP = {1: 1, 2: 2, 3: -3}
PROCESS_ORDER = (2, 3, 1)


def from_behind(value, axis, steps):
    count = lax.axis_size(axis)
    leading, last = (max(0, -steps), min(count, count - steps))
    return lax.ppermute(value, axis, [(source, source + steps) for source in range(leading, last)])


def adjusted_r2(gram_part, samples):
    correl = gram_part / samples
    squared = correl * correl
    return squared - (1.0 - squared) / (samples - 2)


def gram_of(left, right):
    return lax.dot_general(
        left, right, (((0,), (0,)), ((), ())), preferred_element_type=jnp.float32
    )


def reduce_to_owner(part, owner, n_samp):
    pairs_core = [(s, s ^ 1) for s in range(n_samp) if s & 1 != owner & 1]
    summed = part + lax.ppermute(part.astype(jnp.bfloat16), "samp", pairs_core).astype(jnp.float32)
    pairs_chip = [(owner ^ 2, owner)]
    return summed + lax.ppermute(summed.astype(jnp.bfloat16), "samp", pairs_chip).astype(
        jnp.float32
    )


def local(dosages, observed):
    coded = jnp.where(observed != 0, dosages, jnp.asarray(-1, dosages.dtype))
    raw = {
        offset: from_behind(coded, "var", -PARTNER_STEP[offset]) for offset in range(1, BAND + 1)
    }
    values = dosages.astype(jnp.float32)
    present = observed.astype(jnp.float32)
    n_samp = lax.axis_size("samp")
    n_var = lax.axis_size("var")
    position = lax.axis_index("var")
    me = lax.axis_index("samp")
    partial = jnp.stack(
        [jnp.sum(present, 0), jnp.sum(present * values, 0), jnp.sum(present * values * values, 0)]
    )
    slots = jnp.zeros((n_var,) + partial.shape, jnp.float32)
    stats = lax.psum(lax.dynamic_update_index_in_dim(slots, partial, position, 0), ("var", "samp"))
    seen_count = jnp.maximum(stats[:, 0], 1.0)
    column_mean = stats[:, 1] / seen_count
    spread = stats[:, 2] / seen_count - column_mean * column_mean
    inverse_sd = lax.rsqrt(spread + 1e-05)
    own_mean = lax.dynamic_index_in_dim(column_mean, position, 0, keepdims=False)
    own_sd = lax.dynamic_index_in_dim(inverse_sd, position, 0, keepdims=False)
    standard = ((values - own_mean) * own_sd * present).astype(jnp.bfloat16)
    samples = standard.shape[0] * n_samp
    block_width = standard.shape[1]
    owned = {0: reduce_to_owner(gram_of(standard, standard), 0, n_samp)}
    arrived, owned[0] = lax.optimization_barrier(([raw[d] for d in PROCESS_ORDER], owned[0]))
    for offset, coded_partner in zip(PROCESS_ORDER, arrived):
        source = jnp.clip(position + PARTNER_STEP[offset], 0, n_var - 1)
        partner_mean = lax.dynamic_index_in_dim(column_mean, source, 0, keepdims=False)
        partner_sd = lax.dynamic_index_in_dim(inverse_sd, source, 0, keepdims=False)
        partner_values = coded_partner.astype(jnp.float32)
        partner_present = (partner_values >= 0).astype(jnp.float32)
        partner = ((partner_values - partner_mean) * partner_sd * partner_present).astype(
            jnp.bfloat16
        )
        owned[offset] = reduce_to_owner(gram_of(standard, partner), offset, n_samp)
    gram = lax.dynamic_index_in_dim(
        jnp.stack([owned[d] for d in range(BAND + 1)]), me, 0, keepdims=False
    )
    steps = jnp.array([0] + [PARTNER_STEP[d] for d in range(1, BAND + 1)], jnp.int32)
    target = position + steps[me]
    in_range = ((target >= 0) & (target < n_var)).astype(jnp.float32)
    adjusted = adjusted_r2(gram, samples) * in_range
    row_sums = jnp.sum(adjusted, 1)
    col_sums = jnp.sum(adjusted, 0) * (me > 0).astype(jnp.float32)
    pairs = []
    for var_idx in range(n_var):
        for offset in range(1, BAND + 1):
            dest = var_idx + PARTNER_STEP[offset]
            if 0 <= dest < n_var:
                pairs.append((var_idx * n_samp + offset, dest * n_samp + offset))
    moved = lax.ppermute(col_sums, ("var", "samp"), pairs)
    total = lax.psum_scatter(row_sums + moved, "samp", scatter_dimension=0, tiled=True)
    return total / block_width


def solution(mesh):
    placed = (P("samp", "var"), P("samp", "var"))
    return jax.shard_map(
        local, mesh=mesh, in_specs=placed, out_specs=P(("var", "samp")), check_vma=False
    )
```

profile of v0, /device:TPU:0, one launch (start us, length us, event | category | flops | bytes accessed | tf_op | source)
XLA Modules:
  0.0 372.2 jit_solution(16671350342384689641)
XLA Ops:
  6.5 5.4 %fusion.13 = (f32[768]{0:T(1024)S(1)}, f32[768]{0:T(1024)S(1)}, f32[768]{0:T(1024)S(1)}) fusion(bf16[2048,768]{1,0:T(8,128)(2,1)} %param.3, s32[2048,768]{1,0:T(8,128)} %param.4), kind=kLoop, calls=%fused_computation.28 | loop fusion | flops 11007744 | bytes 9446400 | tf_op jit(solution)/shard_map/reduce_sum | solution.py:50
  12.7 5.3 %compare_select_fusion = bf16[2048,768]{1,0:T(8,128)(2,1)} fusion(bf16[2048,768]{1,0:T(8,128)(2,1)S(1)} %copy-done, s32[2048,768]{1,0:T(8,128)} %param.4), kind=kLoop, calls=%fused_computation.27 | loop fusion | flops 3145728 | bytes 12582912 | tf_op jit(solution)/shard_map/jit(_where)/select_n | solution.py:39
  18.0 1.3 collective-permute-start
  19.3 8.7 %collective-permute-start.1 = (bf16[2048,768]{1,0:T(8,128)(2,1)}, bf16[2048,768]{1,0:T(8,128)(2,1)}, u32[]{:S(2)}, u32[]{:S(2)}) collective-permute-start(bf16[2048,768]{1,0:T(8,128)(2,1)} %compare_select_fusion), channel_id=1, source_target_pairs={{0,12},{4,16},{8,20},{12,24},{16,28},{1,13},{5,17},{9,21},{13,25},... | collective-permute-start | bytes 9437192 | tf_op jit(solution)/shard_map/ppermute | solution.py:14
  27.9 1.3 collective-permute-start.2
  29.2 232.4 %all-reduce.3.cloned.1.call-done = f32[8,3,768]{2,1,0:T(4,128)} async-done(((f32[8,3,768]{2,1,0:T(4,128)}), f32[8,3,768]{2,1,0:T(4,128)}) %all-reduce.3.cloned.1.call-update) | async-done | bytes 73744 | tf_op jit(solution)/shard_map/psum | solution.py:53
  261.6 1.1 add_rsqrt_fusion
  262.8 3.9 %fusion.12 = bf16[2048,768]{1,0:T(8,128)(2,1)S(1)} fusion(bf16[2048,768]{1,0:T(8,128)(2,1)S(1)} %copy-done, s32[2048,768]{1,0:T(8,128)} %param.4, f32[768]{0:T(1024)S(1)} %get-tuple-element.37, f32[768]{0:T(1024)S(1)} %get-tuple-element.21), kind=kLoop, calls=%fused_computation.25 | loop fusion | flops 9437184 | bytes 12589056 | tf_op jit(solution)/shard_map/convert_element_type | solution.py:60
  266.8 2.7 fusion.53
  269.5 1.3 collective-permute-start.3
  270.8 3.4 collective-permute-done.3
  274.5 1.3 collective-permute-start.4
  275.8 16.8 %collective-permute-done.4 = bf16[768,768]{1,0:T(8,128)(2,1)S(1)} collective-permute-done((bf16[768,768]{1,0:T(8,128)(2,1)S(1)}, bf16[768,768]{1,0:T(8,128)(2,1)S(1)}, u32[]{:S(2)}, u32[]{:S(2)}) %collective-permute-start.4) | collective-permute-done | bytes 1179680 | tf_op jit(solution)/shard_map/ppermute | solution.py:33
  292.6 1.7 convert_add_fusion.3
  294.3 4.8 %fusion.56 = (bf16[768,768]{1,0:T(8,128)(2,1)S(1)}, f32[768,768]{1,0:T(8,128)S(1)}) fusion(bf16[2048,768]{1,0:T(8,128)(2,1)S(1)} %fusion.12, bf16[2048,768]{1,0:T(8,128)(2,1)} %collective-permute-done.2, f32[768]{0:T(1024)S(1)} %get-tuple-element.39, f32[768]{0:T(1024)S(1)} %get-tuple-element.18), kind=kOutput, calls=%fused_computation.92 | convolution fusion | flops 2425946112 | bytes 9836544 | tf_op jit(solution)/shard_map/dot_general | solution.py:24
  299.1 1.5 collective-permute-start.5
  300.7 4.8 %fusion.55 = (bf16[768,768]{1,0:T(8,128)(2,1)S(1)}, f32[768,768]{1,0:T(8,128)S(1)}) fusion(bf16[2048,768]{1,0:T(8,128)(2,1)S(1)} %fusion.12, bf16[2048,768]{1,0:T(8,128)(2,1)} %collective-permute-done, f32[768]{0:T(1024)S(1)} %get-tuple-element.38, f32[768]{0:T(1024)S(1)} %get-tuple-element.20), kind=kOutput, calls=%fused_computation.91 | convolution fusion | flops 2425946112 | bytes 9836544 | tf_op jit(solution)/shard_map/dot_general | solution.py:24
  305.5 1.3 collective-permute-start.7
  306.8 4.8 %fusion.54 = (bf16[768,768]{1,0:T(8,128)(2,1)S(1)}, f32[768,768]{1,0:T(8,128)S(1)}) fusion(bf16[2048,768]{1,0:T(8,128)(2,1)S(1)} %fusion.12, bf16[2048,768]{1,0:T(8,128)(2,1)} %collective-permute-done.1, f32[768]{0:T(1024)S(1)} %get-tuple-element.36, f32[768]{0:T(1024)S(1)} %get-tuple-element.19), kind=kOutput, calls=%fused_computation.90 | convolution fusion | flops 2425946112 | bytes 9836544 | tf_op jit(solution)/shard_map/dot_general | solution.py:24
  311.7 3.2 collective-permute-start.9
  314.8 1.3 fusion.36
  316.1 1.7 collective-permute-start.6
  317.8 1.4 fusion.37
  319.3 2.5 collective-permute-start.8
  321.8 1.5 fusion.38
  323.2 1.8 collective-permute-start.10
  326.3 1.7 add_bitcast_fusion.2
  328.0 14.3 %collective-permute-done.8 = bf16[768,768]{1,0:T(8,128)(2,1)} collective-permute-done((bf16[768,768]{1,0:T(8,128)(2,1)}, bf16[768,768]{1,0:T(8,128)(2,1)}, u32[]{:S(2)}, u32[]{:S(2)}) %collective-permute-start.8) | collective-permute-done | bytes 1179680 | tf_op jit(solution)/shard_map/ppermute | solution.py:33
  342.4 1.7 add_bitcast_fusion.1
  344.1 1.8 add_bitcast_fusion
  346.1 1.2 fusion.52
  349.2 15.5 %all-reduce = f32[768]{0:T(1024)S(1)} all-reduce(f32[768]{0:T(1024)S(1)} %add.83), channel_id=2, replica_groups=mesh['var'=8,'samp'=4] {'samp'}, use_global_device_ids=true, to_apply=%region_6.7.clone | all-reduce | flops 768 | bytes 6144
  (50 shorter events, 3.8 us)
Async XLA Ops:
  6.5 255.1 %all-reduce.3.cloned.1.call-start = ((), (), s32[]{:S(2)}) async-start(), calls=%async_computation | async-start | bytes 196608 | tf_op jit(solution)/shard_map/psum | solution.py:53
  6.5 6.2 %copy-start = (bf16[2048,768]{1,0:T(8,128)(2,1)S(1)}, bf16[2048,768]{1,0:T(8,128)(2,1)}, u32[]{:S(2)}) copy-start(bf16[2048,768]{1,0:T(8,128)(2,1)} %param.3) | copy-start | bytes 9437188
  12.0 0.6 copy-start.10
  18.0 276.4 %collective-permute-start = (bf16[2048,768]{1,0:T(8,128)(2,1)}, bf16[2048,768]{1,0:T(8,128)(2,1)}, u32[]{:S(2)}, u32[]{:S(2)}) collective-permute-start(bf16[2048,768]{1,0:T(8,128)(2,1)} %compare_select_fusion), channel_id=1, source_target_pairs={{8,0},{12,4},{16,8},{20,12},{24,16},{28,20},{9,1},{13,5},{17,9},{2... | collective-permute-start | bytes 9437192 | tf_op jit(solution)/shard_map/ppermute | solution.py:14
  19.3 275.1 %collective-permute-start.1 = (bf16[2048,768]{1,0:T(8,128)(2,1)}, bf16[2048,768]{1,0:T(8,128)(2,1)}, u32[]{:S(2)}, u32[]{:S(2)}) collective-permute-start(bf16[2048,768]{1,0:T(8,128)(2,1)} %compare_select_fusion), channel_id=1, source_target_pairs={{0,12},{4,16},{8,20},{12,24},{16,28},{1,13},{5,17},{9,21},{13,25},... | collective-permute-start | bytes 9437192 | tf_op jit(solution)/shard_map/ppermute | solution.py:14
  27.9 266.4 %collective-permute-start.2 = (bf16[2048,768]{1,0:T(8,128)(2,1)}, bf16[2048,768]{1,0:T(8,128)(2,1)}, u32[]{:S(2)}, u32[]{:S(2)}) collective-permute-start(bf16[2048,768]{1,0:T(8,128)(2,1)} %compare_select_fusion), channel_id=1, source_target_pairs={{4,0},{8,4},{12,8},{16,12},{20,16},{24,20},{28,24},{5,1},{9,5},{13... | collective-permute-start | bytes 9437192 | tf_op jit(solution)/shard_map/ppermute | solution.py:14
  269.5 4.7 %collective-permute-start.3 = (bf16[768,768]{1,0:T(8,128)(2,1)S(1)}, bf16[768,768]{1,0:T(8,128)(2,1)S(1)}, u32[]{:S(2)}, u32[]{:S(2)}) collective-permute-start(bf16[768,768]{1,0:T(8,128)(2,1)S(1)} %get-tuple-element.28), channel_id=1, source_target_pairs={{1,0},{3,2},{5,4},{7,6},{9,8},{11,10},{13,12},{15,14},{17,16},{19,... | collective-permute-start | bytes 3538952 | tf_op jit(solution)/shard_map/ppermute | solution.py:31
  274.5 18.1 %collective-permute-start.4 = (bf16[768,768]{1,0:T(8,128)(2,1)S(1)}, bf16[768,768]{1,0:T(8,128)(2,1)S(1)}, u32[]{:S(2)}, u32[]{:S(2)}) collective-permute-start(bf16[768,768]{1,0:T(8,128)(2,1)S(1)} %fusion.35), channel_id=1, source_target_pairs={{2,0},{6,4},{10,8},{14,12},{18,16},{22,20},{26,24},{30,28}} | collective-permute-start | bytes 3538952 | tf_op jit(solution)/shard_map/ppermute | solution.py:33
  299.1 15.7 %collective-permute-start.5 = (bf16[768,768]{1,0:T(8,128)(2,1)S(1)}, bf16[768,768]{1,0:T(8,128)(2,1)S(1)}, u32[]{:S(2)}, u32[]{:S(2)}) collective-permute-start(bf16[768,768]{1,0:T(8,128)(2,1)S(1)} %get-tuple-element.34), channel_id=1, source_target_pairs={{0,1},{2,3},{4,5},{6,7},{8,9},{10,11},{12,13},{14,15},{16,17},{18,... | collective-permute-start | bytes 3538952 | tf_op jit(solution)/shard_map/ppermute | solution.py:31
  305.5 12.3 %copy-start.1 = (f32[768,768]{1,0:T(8,128)}, f32[768,768]{1,0:T(8,128)S(1)}, u32[]{:S(2)}) copy-start(f32[768,768]{1,0:T(8,128)S(1)} %get-tuple-element.33) | copy-start | bytes 7077892
  305.5 12.3 %collective-permute-start.7 = (bf16[768,768]{1,0:T(8,128)(2,1)S(1)}, bf16[768,768]{1,0:T(8,128)(2,1)S(1)}, u32[]{:S(2)}, u32[]{:S(2)}) collective-permute-start(bf16[768,768]{1,0:T(8,128)(2,1)S(1)} %get-tuple-element.32), channel_id=1, source_target_pairs={{1,0},{3,2},{5,4},{7,6},{9,8},{11,10},{13,12},{15,14},{17,16},{19,... | collective-permute-start | bytes 3538952 | tf_op jit(solution)/shard_map/ppermute | solution.py:31
  311.7 10.1 %copy-start.3 = (f32[768,768]{1,0:T(8,128)}, f32[768,768]{1,0:T(8,128)S(1)}, u32[]{:S(2)}) copy-start(f32[768,768]{1,0:T(8,128)S(1)} %get-tuple-element.31) | copy-start | bytes 7077892
  311.7 10.1 %collective-permute-start.9 = (bf16[768,768]{1,0:T(8,128)(2,1)S(1)}, bf16[768,768]{1,0:T(8,128)(2,1)S(1)}, u32[]{:S(2)}, u32[]{:S(2)}) collective-permute-start(bf16[768,768]{1,0:T(8,128)(2,1)S(1)} %get-tuple-element.30), channel_id=1, source_target_pairs={{0,1},{2,3},{4,5},{6,7},{8,9},{10,11},{12,13},{14,15},{16,17},{18,... | collective-permute-start | bytes 3538952 | tf_op jit(solution)/shard_map/ppermute | solution.py:31
  316.1 10.1 %collective-permute-start.6 = (bf16[768,768]{1,0:T(8,128)(2,1)}, bf16[768,768]{1,0:T(8,128)(2,1)}, u32[]{:S(2)}, u32[]{:S(2)}) collective-permute-start(bf16[768,768]{1,0:T(8,128)(2,1)} %fusion.36), channel_id=1, source_target_pairs={{3,1},{7,5},{11,9},{15,13},{19,17},{23,21},{27,25},{31,29}} | collective-permute-start | bytes 3538952 | tf_op jit(solution)/shard_map/ppermute | solution.py:33
  317.8 1.4 copy-start.6
  319.3 23.1 %collective-permute-start.8 = (bf16[768,768]{1,0:T(8,128)(2,1)}, bf16[768,768]{1,0:T(8,128)(2,1)}, u32[]{:S(2)}, u32[]{:S(2)}) collective-permute-start(bf16[768,768]{1,0:T(8,128)(2,1)} %fusion.37), channel_id=1, source_target_pairs={{0,2},{4,6},{8,10},{12,14},{16,18},{20,22},{24,26},{28,30}} | collective-permute-start | bytes 3538952 | tf_op jit(solution)/shard_map/ppermute | solution.py:33
  321.7 1.5 copy-start.8
  321.7 3.3 copy-start.12
  323.2 20.8 %collective-permute-start.10 = (bf16[768,768]{1,0:T(8,128)(2,1)}, bf16[768,768]{1,0:T(8,128)(2,1)}, u32[]{:S(2)}, u32[]{:S(2)}) collective-permute-start(bf16[768,768]{1,0:T(8,128)(2,1)} %fusion.38), channel_id=1, source_target_pairs={{1,3},{5,7},{9,11},{13,15},{17,19},{21,23},{25,27},{29,31}} | collective-permute-start | bytes 3538952 | tf_op jit(solution)/shard_map/ppermute | solution.py:33
  326.2 16.1 %copy-start.2 = (f32[768,768]{1,0:T(8,128)S(1)}, f32[768,768]{1,0:T(8,128)}, u32[]{:S(2)}) copy-start(f32[768,768]{1,0:T(8,128)} %copy-done.1) | copy-start | bytes 7077892
  326.3 16.1 %copy-start.7 = (bf16[768,768]{1,0:T(8,128)(2,1)S(1)}, bf16[768,768]{1,0:T(8,128)(2,1)}, u32[]{:S(2)}) copy-start(bf16[768,768]{1,0:T(8,128)(2,1)} %copy-done.6) | copy-start | bytes 3538948
  328.0 16.0 %copy-start.4 = (f32[768,768]{1,0:T(8,128)S(1)}, f32[768,768]{1,0:T(8,128)}, u32[]{:S(2)}) copy-start(f32[768,768]{1,0:T(8,128)} %copy-done.3) | copy-start | bytes 7077892
  328.0 16.0 %copy-start.9 = (bf16[768,768]{1,0:T(8,128)(2,1)S(1)}, bf16[768,768]{1,0:T(8,128)(2,1)}, u32[]{:S(2)}) copy-start(bf16[768,768]{1,0:T(8,128)(2,1)} %copy-done.8) | copy-start | bytes 3538948
  344.0 2.0 copy-start.5
  346.1 1.9 copy-start.11
  347.3 1.9 collective-permute-start.11
Sparse Core Ops, SparseCore 0:
  12.9 248.6 all-reduce.2
where the time goes:
time: 373 us; the launch traced here: 372 us
  waiting for transfers between devices  267 us (72%)
  other arithmetic  29 us (8%)
  starting transfers between devices  26.4 us (7%)
  matrix products  17.2 us (5%)
  blocking collectives  15.5 us (4%)
  between operations  15 us (4%)
    psum x1, waiting for transfers between devices, local(): lax.psum(lax.dynamic_update_index_in_dim(slots, partial, position, 0), ('...  232 us
    ppermute x4, waiting for transfers between devices, reduce_to_owner(): lax.ppermute(summed.astype(jnp.bfloat16), 'samp', pairs_chip)  31.1 us
    dot_general x4, matrix products, gram_of(): lax.dot_general(left, right, (((0,), (0,)), ((), ())), preferred_element_...  17.2 us
    unnamed x1, blocking collectives  15.5 us
    ppermute x3, starting transfers between devices, from_behind(): lax.ppermute(value, axis, [(source, source + steps) for source in range(l...  11.2 us
  transfers between devices with their start and end apart: 13, of which 4 were waited for; matrix products, arithmetic and copies ran while one was open for 9% of the time, Pallas kernels for 0%

commit v1 on v0

--- a/solution.py
+++ b/solution.py
@@ -50,7 +50,12 @@
         [jnp.sum(present, 0), jnp.sum(present * values, 0), jnp.sum(present * values * values, 0)]
     )
     slots = jnp.zeros((n_var,) + partial.shape, jnp.float32)
-    stats = lax.psum(lax.dynamic_update_index_in_dim(slots, partial, position, 0), ("var", "samp"))
+    stats = jnp.sum(
+        lax.all_gather(
+            lax.dynamic_update_index_in_dim(slots, partial, position, 0), ("var", "samp")
+        ),
+        axis=0,
+    )
     seen_count = jnp.maximum(stats[:, 0], 1.0)
     column_mean = stats[:, 1] / seen_count
     spread = stats[:, 2] / seen_count - column_mean * column_mean

time: 373 us -> 299 us (0.80)
  waiting for transfers between devices: 267 us -> 194 us
    psum x1 -> x0, waiting for transfers between devices: 232 us -> none  [local(): lax.psum(lax.dynamic_update_index_in_dim(slots, partial, position, 0), ('...]
    all_gather x0 -> x1, waiting for transfers between devices: none -> 159 us  [local(): lax.all_gather(lax.dynamic_update_index_in_dim(slots, partial, position,...]
  transfers between devices with their start and end apart: 13 -> 13, of which waited for: 4 -> 4; matrix products, arithmetic and copies ran while one was open for 9% -> 11% of each run, Pallas kernels for 0% -> 0%
where the time goes in v1:
time: 299 us; the launch traced here: 298 us
  waiting for transfers between devices  194 us (65%)
  other arithmetic  29.7 us (10%)
  starting transfers between devices  26.4 us (9%)
  matrix products  17.1 us (6%)
  between operations  15.1 us (5%)
  blocking collectives  13.8 us (5%)
    all_gather x1, waiting for transfers between devices, local(): lax.all_gather(lax.dynamic_update_index_in_dim(slots, partial, position,...  159 us
    ppermute x4, waiting for transfers between devices, reduce_to_owner(): lax.ppermute(summed.astype(jnp.bfloat16), 'samp', pairs_chip)  31.1 us
    dot_general x4, matrix products, gram_of(): lax.dot_general(left, right, (((0,), (0,)), ((), ())), preferred_element_...  17.1 us
    unnamed x1, blocking collectives  13.8 us
    ppermute x3, starting transfers between devices, from_behind(): lax.ppermute(value, axis, [(source, source + steps) for source in range(l...  11.2 us
    ppermute x4, starting transfers between devices, reduce_to_owner(): lax.ppermute(part.astype(jnp.bfloat16), 'samp', pairs_core)  7.29 us
    ppermute x4, starting transfers between devices, reduce_to_owner(): lax.ppermute(summed.astype(jnp.bfloat16), 'samp', pairs_chip)  7.23 us
  transfers between devices with their start and end apart: 13, of which 4 were waited for; matrix products, arithmetic and copies ran while one was open for 11% of the time, Pallas kernels for 0%

profile of v1, /device:TPU:0, one launch (start us, length us, event | category | flops | bytes accessed | tf_op | source)
XLA Modules:
  0.0 298.3 jit_solution(7848624113319050425)
XLA Ops:
  6.5 5.4 %fusion.13 = (f32[768]{0:T(1024)S(1)}, f32[768]{0:T(1024)S(1)}, f32[768]{0:T(1024)S(1)}) fusion(bf16[2048,768]{1,0:T(8,128)(2,1)} %param.3, s32[2048,768]{1,0:T(8,128)} %param.4), kind=kLoop, calls=%fused_computation.28 | loop fusion | flops 11007744 | bytes 9446400 | tf_op jit(solution)/shard_map/reduce_sum | solution.py:50
  12.8 5.3 %compare_select_fusion = bf16[2048,768]{1,0:T(8,128)(2,1)} fusion(bf16[2048,768]{1,0:T(8,128)(2,1)S(1)} %copy-done, s32[2048,768]{1,0:T(8,128)} %param.4), kind=kLoop, calls=%fused_computation.27 | loop fusion | flops 3145728 | bytes 12582912 | tf_op jit(solution)/shard_map/jit(_where)/select_n | solution.py:39
  18.1 1.3 collective-permute-start
  19.4 8.7 %collective-permute-start.1 = (bf16[2048,768]{1,0:T(8,128)(2,1)}, bf16[2048,768]{1,0:T(8,128)(2,1)}, u32[]{:S(2)}, u32[]{:S(2)}) collective-permute-start(bf16[2048,768]{1,0:T(8,128)(2,1)} %compare_select_fusion), channel_id=1, source_target_pairs={{0,12},{4,16},{8,20},{12,24},{16,28},{1,13},{5,17},{9,21},{13,25},... | collective-permute-start | bytes 9437192 | tf_op jit(solution)/shard_map/ppermute | solution.py:14
  28.1 1.3 collective-permute-start.2
  29.4 159.3 %all-gather.2.cloned.1.call-done = f32[32,8,3,768]{3,1,2,0:T(8,128)} async-done(((f32[1,8,3,768]{3,1,2,0:T(8,128)}), f32[32,8,3,768]{3,1,2,0:T(8,128)}) %all-gather.2.cloned.1.call-update) | async-done | bytes 2359312 | tf_op jit(solution)/shard_map/all_gather | solution.py:54
  188.7 1.8 reduce_sum.57
  190.6 3.9 %fusion.12 = bf16[2048,768]{1,0:T(8,128)(2,1)S(1)} fusion(bf16[2048,768]{1,0:T(8,128)(2,1)S(1)} %copy-done, s32[2048,768]{1,0:T(8,128)} %param.4, f32[768]{0:T(1024)S(1)} %get-tuple-element.24, f32[768]{0:T(1024)S(1)} %get-tuple-element.36), kind=kLoop, calls=%fused_computation.25 | loop fusion | flops 9437184 | bytes 12589056 | tf_op jit(solution)/shard_map/convert_element_type | solution.py:65
  194.5 2.7 fusion.46
  197.2 1.3 collective-permute-start.3
  198.5 3.4 %collective-permute-done.3 = bf16[768,768]{1,0:T(8,128)(2,1)S(1)} collective-permute-done((bf16[768,768]{1,0:T(8,128)(2,1)S(1)}, bf16[768,768]{1,0:T(8,128)(2,1)S(1)}, u32[]{:S(2)}, u32[]{:S(2)}) %collective-permute-start.3) | collective-permute-done | bytes 1179680 | tf_op jit(solution)/shard_map/ppermute | solution.py:31
  202.3 1.3 collective-permute-start.4
  203.6 16.8 %collective-permute-done.4 = bf16[768,768]{1,0:T(8,128)(2,1)S(1)} collective-permute-done((bf16[768,768]{1,0:T(8,128)(2,1)S(1)}, bf16[768,768]{1,0:T(8,128)(2,1)S(1)}, u32[]{:S(2)}, u32[]{:S(2)}) %collective-permute-start.4) | collective-permute-done | bytes 1179680 | tf_op jit(solution)/shard_map/ppermute | solution.py:33
  220.4 1.7 convert_add_fusion.3
  222.1 4.8 %fusion.49 = (bf16[768,768]{1,0:T(8,128)(2,1)S(1)}, f32[768,768]{1,0:T(8,128)S(1)}) fusion(bf16[2048,768]{1,0:T(8,128)(2,1)S(1)} %fusion.12, bf16[2048,768]{1,0:T(8,128)(2,1)} %collective-permute-done.2, f32[768]{0:T(1024)S(1)} %get-tuple-element.22, f32[768]{0:T(1024)S(1)} %get-tuple-element.39), kind=kOutput, calls=%fused_computation.84 | convolution fusion | flops 2425946112 | bytes 9836544 | tf_op jit(solution)/shard_map/dot_general | solution.py:24
  226.9 1.5 collective-permute-start.5
  228.4 4.8 %fusion.48 = (bf16[768,768]{1,0:T(8,128)(2,1)S(1)}, f32[768,768]{1,0:T(8,128)S(1)}) fusion(bf16[2048,768]{1,0:T(8,128)(2,1)S(1)} %fusion.12, bf16[2048,768]{1,0:T(8,128)(2,1)} %collective-permute-done, f32[768]{0:T(1024)S(1)} %get-tuple-element.23, f32[768]{0:T(1024)S(1)} %get-tuple-element.37), kind=kOutput, calls=%fused_computation.83 | convolution fusion | flops 2425946112 | bytes 9836544 | tf_op jit(solution)/shard_map/dot_general | solution.py:24
  233.3 1.3 collective-permute-start.7
  234.6 4.8 %fusion.47 = (bf16[768,768]{1,0:T(8,128)(2,1)S(1)}, f32[768,768]{1,0:T(8,128)S(1)}) fusion(bf16[2048,768]{1,0:T(8,128)(2,1)S(1)} %fusion.12, bf16[2048,768]{1,0:T(8,128)(2,1)} %collective-permute-done.1, f32[768]{0:T(1024)S(1)} %get-tuple-element.25, f32[768]{0:T(1024)S(1)} %get-tuple-element.38), kind=kOutput, calls=%fused_computation.82 | convolution fusion | flops 2425946112 | bytes 9836544 | tf_op jit(solution)/shard_map/dot_general | solution.py:24
  239.4 3.2 %collective-permute-start.9 = (bf16[768,768]{1,0:T(8,128)(2,1)S(1)}, bf16[768,768]{1,0:T(8,128)(2,1)S(1)}, u32[]{:S(2)}, u32[]{:S(2)}) collective-permute-start(bf16[768,768]{1,0:T(8,128)(2,1)S(1)} %get-tuple-element.30), channel_id=1, source_target_pairs={{0,1},{2,3},{4,5},{6,7},{8,9},{10,11},{12,13},{14,15},{16,17},{18,... | collective-permute-start | bytes 3538952 | tf_op jit(solution)/shard_map/ppermute | solution.py:31
  242.6 1.3 fusion.36
  243.9 1.7 collective-permute-start.6
  245.6 1.4 fusion.37
  247.0 2.5 collective-permute-start.8
  249.5 1.5 fusion.38
  251.0 1.8 collective-permute-start.10
  254.0 1.7 add_bitcast_fusion.2
  255.8 14.3 %collective-permute-done.8 = bf16[768,768]{1,0:T(8,128)(2,1)} collective-permute-done((bf16[768,768]{1,0:T(8,128)(2,1)}, bf16[768,768]{1,0:T(8,128)(2,1)}, u32[]{:S(2)}, u32[]{:S(2)}) %collective-permute-start.8) | collective-permute-done | bytes 1179680 | tf_op jit(solution)/shard_map/ppermute | solution.py:33
  270.1 1.7 add_bitcast_fusion.1
  271.8 1.8 add_bitcast_fusion
  273.8 1.2 fusion.45
  277.0 13.8 %all-reduce = f32[768]{0:T(1024)S(1)} all-reduce(f32[768]{0:T(1024)S(1)} %add.81), channel_id=2, replica_groups=mesh['var'=8,'samp'=4] {'samp'}, use_global_device_ids=true, to_apply=%region_6.7.clone | all-reduce | flops 768 | bytes 6144
  (53 shorter events, 3.9 us)
Async XLA Ops:
  6.5 182.2 %all-gather.2.cloned.1.call-start = ((), (), s32[]{:S(2)}) async-start(), calls=%async_computation | async-start | bytes 2433024 | tf_op jit(solution)/shard_map/all_gather | solution.py:54
  6.5 6.3 %copy-start = (bf16[2048,768]{1,0:T(8,128)(2,1)S(1)}, bf16[2048,768]{1,0:T(8,128)(2,1)}, u32[]{:S(2)}) copy-start(bf16[2048,768]{1,0:T(8,128)(2,1)} %param.3) | copy-start | bytes 9437188
  12.2 0.6 copy-start.10
  18.1 204.0 %collective-permute-start = (bf16[2048,768]{1,0:T(8,128)(2,1)}, bf16[2048,768]{1,0:T(8,128)(2,1)}, u32[]{:S(2)}, u32[]{:S(2)}) collective-permute-start(bf16[2048,768]{1,0:T(8,128)(2,1)} %compare_select_fusion), channel_id=1, source_target_pairs={{8,0},{12,4},{16,8},{20,12},{24,16},{28,20},{9,1},{13,5},{17,9},{2... | collective-permute-start | bytes 9437192 | tf_op jit(solution)/shard_map/ppermute | solution.py:14
  19.4 202.7 %collective-permute-start.1 = (bf16[2048,768]{1,0:T(8,128)(2,1)}, bf16[2048,768]{1,0:T(8,128)(2,1)}, u32[]{:S(2)}, u32[]{:S(2)}) collective-permute-start(bf16[2048,768]{1,0:T(8,128)(2,1)} %compare_select_fusion), channel_id=1, source_target_pairs={{0,12},{4,16},{8,20},{12,24},{16,28},{1,13},{5,17},{9,21},{13,25},... | collective-permute-start | bytes 9437192 | tf_op jit(solution)/shard_map/ppermute | solution.py:14
  28.1 194.0 %collective-permute-start.2 = (bf16[2048,768]{1,0:T(8,128)(2,1)}, bf16[2048,768]{1,0:T(8,128)(2,1)}, u32[]{:S(2)}, u32[]{:S(2)}) collective-permute-start(bf16[2048,768]{1,0:T(8,128)(2,1)} %compare_select_fusion), channel_id=1, source_target_pairs={{4,0},{8,4},{12,8},{16,12},{20,16},{24,20},{28,24},{5,1},{9,5},{13... | collective-permute-start | bytes 9437192 | tf_op jit(solution)/shard_map/ppermute | solution.py:14
  197.2 4.7 %collective-permute-start.3 = (bf16[768,768]{1,0:T(8,128)(2,1)S(1)}, bf16[768,768]{1,0:T(8,128)(2,1)S(1)}, u32[]{:S(2)}, u32[]{:S(2)}) collective-permute-start(bf16[768,768]{1,0:T(8,128)(2,1)S(1)} %get-tuple-element.28), channel_id=1, source_target_pairs={{1,0},{3,2},{5,4},{7,6},{9,8},{11,10},{13,12},{15,14},{17,16},{19,... | collective-permute-start | bytes 3538952 | tf_op jit(solution)/shard_map/ppermute | solution.py:31
  202.3 18.1 %collective-permute-start.4 = (bf16[768,768]{1,0:T(8,128)(2,1)S(1)}, bf16[768,768]{1,0:T(8,128)(2,1)S(1)}, u32[]{:S(2)}, u32[]{:S(2)}) collective-permute-start(bf16[768,768]{1,0:T(8,128)(2,1)S(1)} %fusion.35), channel_id=1, source_target_pairs={{2,0},{6,4},{10,8},{14,12},{18,16},{22,20},{26,24},{30,28}} | collective-permute-start | bytes 3538952 | tf_op jit(solution)/shard_map/ppermute | solution.py:33
  226.9 15.7 %collective-permute-start.5 = (bf16[768,768]{1,0:T(8,128)(2,1)S(1)}, bf16[768,768]{1,0:T(8,128)(2,1)S(1)}, u32[]{:S(2)}, u32[]{:S(2)}) collective-permute-start(bf16[768,768]{1,0:T(8,128)(2,1)S(1)} %get-tuple-element.34), channel_id=1, source_target_pairs={{0,1},{2,3},{4,5},{6,7},{8,9},{10,11},{12,13},{14,15},{16,17},{18,... | collective-permute-start | bytes 3538952 | tf_op jit(solution)/shard_map/ppermute | solution.py:31
  233.3 12.3 %copy-start.1 = (f32[768,768]{1,0:T(8,128)}, f32[768,768]{1,0:T(8,128)S(1)}, u32[]{:S(2)}) copy-start(f32[768,768]{1,0:T(8,128)S(1)} %get-tuple-element.33) | copy-start | bytes 7077892
  233.3 12.3 %collective-permute-start.7 = (bf16[768,768]{1,0:T(8,128)(2,1)S(1)}, bf16[768,768]{1,0:T(8,128)(2,1)S(1)}, u32[]{:S(2)}, u32[]{:S(2)}) collective-permute-start(bf16[768,768]{1,0:T(8,128)(2,1)S(1)} %get-tuple-element.32), channel_id=1, source_target_pairs={{1,0},{3,2},{5,4},{7,6},{9,8},{11,10},{13,12},{15,14},{17,16},{19,... | collective-permute-start | bytes 3538952 | tf_op jit(solution)/shard_map/ppermute | solution.py:31
  239.4 10.1 %copy-start.3 = (f32[768,768]{1,0:T(8,128)}, f32[768,768]{1,0:T(8,128)S(1)}, u32[]{:S(2)}) copy-start(f32[768,768]{1,0:T(8,128)S(1)} %get-tuple-element.31) | copy-start | bytes 7077892
  239.4 10.1 %collective-permute-start.9 = (bf16[768,768]{1,0:T(8,128)(2,1)S(1)}, bf16[768,768]{1,0:T(8,128)(2,1)S(1)}, u32[]{:S(2)}, u32[]{:S(2)}) collective-permute-start(bf16[768,768]{1,0:T(8,128)(2,1)S(1)} %get-tuple-element.30), channel_id=1, source_target_pairs={{0,1},{2,3},{4,5},{6,7},{8,9},{10,11},{12,13},{14,15},{16,17},{18,... | collective-permute-start | bytes 3538952 | tf_op jit(solution)/shard_map/ppermute | solution.py:31
  243.9 10.1 %collective-permute-start.6 = (bf16[768,768]{1,0:T(8,128)(2,1)}, bf16[768,768]{1,0:T(8,128)(2,1)}, u32[]{:S(2)}, u32[]{:S(2)}) collective-permute-start(bf16[768,768]{1,0:T(8,128)(2,1)} %fusion.36), channel_id=1, source_target_pairs={{3,1},{7,5},{11,9},{15,13},{19,17},{23,21},{27,25},{31,29}} | collective-permute-start | bytes 3538952 | tf_op jit(solution)/shard_map/ppermute | solution.py:33
  245.6 1.4 copy-start.6
  247.0 23.1 %collective-permute-start.8 = (bf16[768,768]{1,0:T(8,128)(2,1)}, bf16[768,768]{1,0:T(8,128)(2,1)}, u32[]{:S(2)}, u32[]{:S(2)}) collective-permute-start(bf16[768,768]{1,0:T(8,128)(2,1)} %fusion.37), channel_id=1, source_target_pairs={{0,2},{4,6},{8,10},{12,14},{16,18},{20,22},{24,26},{28,30}} | collective-permute-start | bytes 3538952 | tf_op jit(solution)/shard_map/ppermute | solution.py:33
  249.5 1.5 copy-start.8
  249.5 3.3 %copy-start.12 = (s32[4]{0:T(128)S(1)}, s32[4]{0:T(128)}, u32[]{:S(2)}) copy-start(s32[4]{0:T(128)} %constant.83.clone) | copy-start | bytes 52
  251.0 20.8 %collective-permute-start.10 = (bf16[768,768]{1,0:T(8,128)(2,1)}, bf16[768,768]{1,0:T(8,128)(2,1)}, u32[]{:S(2)}, u32[]{:S(2)}) collective-permute-start(bf16[768,768]{1,0:T(8,128)(2,1)} %fusion.38), channel_id=1, source_target_pairs={{1,3},{5,7},{9,11},{13,15},{17,19},{21,23},{25,27},{29,31}} | collective-permute-start | bytes 3538952 | tf_op jit(solution)/shard_map/ppermute | solution.py:33
  254.0 16.1 %copy-start.2 = (f32[768,768]{1,0:T(8,128)S(1)}, f32[768,768]{1,0:T(8,128)}, u32[]{:S(2)}) copy-start(f32[768,768]{1,0:T(8,128)} %copy-done.1) | copy-start | bytes 7077892
  254.0 16.1 %copy-start.7 = (bf16[768,768]{1,0:T(8,128)(2,1)S(1)}, bf16[768,768]{1,0:T(8,128)(2,1)}, u32[]{:S(2)}) copy-start(bf16[768,768]{1,0:T(8,128)(2,1)} %copy-done.6) | copy-start | bytes 3538948
  255.8 16.0 %copy-start.4 = (f32[768,768]{1,0:T(8,128)S(1)}, f32[768,768]{1,0:T(8,128)}, u32[]{:S(2)}) copy-start(f32[768,768]{1,0:T(8,128)} %copy-done.3) | copy-start | bytes 7077892
  255.8 16.0 %copy-start.9 = (bf16[768,768]{1,0:T(8,128)(2,1)S(1)}, bf16[768,768]{1,0:T(8,128)(2,1)}, u32[]{:S(2)}) copy-start(bf16[768,768]{1,0:T(8,128)(2,1)} %copy-done.8) | copy-start | bytes 3538948
  271.8 2.0 copy-start.5
  273.8 1.9 copy-start.11
  275.1 1.9 collective-permute-start.11
Sparse Core Ops, SparseCore 0:
  12.9 175.7 all-gather.1
